TPU v7x, 128 devices: a whole 4x4x4 slice. The times are simulated.
128 devices in a mesh: dp: 8 (over x, core), pair: 16 (over z, y).
Axes of the slice: x: 4, y: 4, z: 4, core: 2. Of those that a mesh axis runs over, the one named last changes fastest.
Arguments:
- anchor: bfloat16 [5, 4096, 1024], P(None, ('dp', 'pair')), may hold values from -20 to 20
- partner: bfloat16 [5, 4096, 1024], P(None, ('dp', 'pair')), may hold values from -12 to 12
- counts: int32 [5], replicated, may hold values from 512 to 4096, as said below
- pair_scale: float32 [5], replicated, may hold values from 2 to 8
Outputs:
- loss_value: float32 [], replicated
- grad_anchor: float32 [5, 4096, 1024], P(None, ('dp', 'pair'))
- grad_partner: float32 [5, 4096, 1024], P(None, ('dp', 'pair'))
Inputs may be any that keep to these rules, and one draw needn't show every extreme that they name: The valid samples of pair p are its rows 0 to counts[p] - 1; one pair has all 4096 rows valid.
All inputs are finite; a program needn't handle non-finite values.
Results may differ from a plain program's by a relative error of at most 0.0021.
Values may be sent and summed in bfloat16 or wider, within the bound.
No kernel may reach another device: no remote copies, remote signals or barrier semaphores. Data moves between devices by JAX's collectives and lax.ppermute only.
A program may use at most 128 MiB of HBM per device.

v0:
```python
import math
import jax
import jax.numpy as jnp
from jax import lax
from jax.sharding import PartitionSpec as P

NEG = -1e30


def merge_gathered(stats):
    highs = stats[:, 0]
    sums = stats[:, 1]
    highest = jnp.max(highs, axis=0)
    summed = jnp.sum(sums * jnp.exp(highs - highest[None]), axis=0)
    return (highest, summed)


def per_device(anchor, partner, counts, pair_scale):
    pair_count, shard_rows, model_width = anchor.shape
    score_scale = 4.0 / math.sqrt(model_width)
    dp_size = lax.axis_size("dp")
    pair_size = lax.axis_size("pair")
    dp_index = lax.axis_index("dp")
    pair_place = lax.axis_index("pair")
    own_first = (dp_index * pair_size + pair_place) * shard_rows
    row_set = lax.all_gather(anchor, "pair", axis=1, tiled=True)
    col_set = lax.all_gather(partner, "dp", axis=1, tiled=True)
    row_count = row_set.shape[1]
    offsets = jnp.arange(shard_rows, dtype=jnp.int32)
    row_global = dp_index * row_count + jnp.arange(row_count, dtype=jnp.int32)
    col_first = (jnp.arange(dp_size, dtype=jnp.int32) * pair_size + pair_place) * shard_rows
    col_global = (col_first[:, None] + offsets[None, :]).reshape(-1)
    row_valid = row_global[None, :] < counts[:, None]
    col_valid = col_global[None, :] < counts[:, None]
    inside = row_valid[:, :, None] & col_valid[:, None, :]
    scores = (
        jnp.einsum("prd,pcd->prc", row_set, col_set, preferred_element_type=jnp.float32)
        * score_scale
    )
    masked = jnp.where(inside, scores, NEG)
    row_high = jnp.max(masked, axis=2)
    row_sum = jnp.sum(jnp.where(inside, jnp.exp(masked - row_high[:, :, None]), 0.0), axis=2)
    col_high = jnp.max(masked, axis=1)
    col_sum = jnp.sum(jnp.where(inside, jnp.exp(masked - col_high[:, None, :]), 0.0), axis=1)
    row_stats = lax.all_gather(jnp.stack([row_high, row_sum]), "pair")
    col_stats = lax.all_gather(jnp.stack([col_high, col_sum]), "dp")
    row_high, row_sum = merge_gathered(row_stats)
    col_high, col_sum = merge_gathered(col_stats)
    row_lse = jnp.where(row_valid, row_high + jnp.log(jnp.where(row_valid, row_sum, 1.0)), 0.0)
    col_lse = jnp.where(col_valid, col_high + jnp.log(jnp.where(col_valid, col_sum, 1.0)), 0.0)
    own_valid = own_first + offsets[None, :] < counts[:, None]
    row_own = lax.dynamic_slice_in_dim(row_lse, pair_place * shard_rows, shard_rows, 1)
    col_own = lax.dynamic_slice_in_dim(col_lse, dp_index * shard_rows, shard_rows, 1)
    positive = (
        jnp.sum(anchor.astype(jnp.float32) * partner.astype(jnp.float32), axis=2) * score_scale
    )
    loss_terms = jnp.where(own_valid, row_own + col_own - 2.0 * positive, 0.0)
    totals = lax.psum(jnp.sum(loss_terms, axis=1), ("dp", "pair"))
    loss_value = jnp.sum(totals / (2.0 * counts.astype(jnp.float32))) / pair_count
    prob_row = jnp.where(inside, jnp.exp(scores - row_lse[:, :, None]), 0.0)
    prob_col = jnp.where(inside, jnp.exp(scores - col_lse[:, None, :]), 0.0)
    weights = (pair_scale[:, None, None] * 0.5 * (prob_row + prob_col)).astype(jnp.bfloat16)
    grad_rows = (
        jnp.einsum("prc,pcd->prd", weights, col_set, preferred_element_type=jnp.float32)
        * score_scale
    )
    grad_cols = (
        jnp.einsum("prc,prd->pcd", weights, row_set, preferred_element_type=jnp.float32)
        * score_scale
    )
    anchor_part = lax.psum_scatter(grad_rows, "pair", scatter_dimension=1, tiled=True)
    partner_part = lax.psum_scatter(grad_cols, "dp", scatter_dimension=1, tiled=True)
    own_term = (pair_scale * score_scale)[:, None, None]
    keep_rows = own_valid[:, :, None]
    anchor_out = jnp.where(keep_rows, anchor_part - own_term * partner.astype(jnp.float32), 0.0)
    partner_out = jnp.where(keep_rows, partner_part - own_term * anchor.astype(jnp.float32), 0.0)
    return (loss_value, anchor_out, partner_out)


def solution(mesh):
    in_specs = (P(None, ("dp", "pair"), None), P(None, ("dp", "pair"), None), P(), P())
    out_specs = (P(), P(None, ("dp", "pair"), None), P(None, ("dp", "pair"), None))
    return jax.shard_map(
        per_device, mesh=mesh, in_specs=in_specs, out_specs=out_specs, check_vma=False
    )
```

profile of v0, /device:TPU:1, one launch (start us, length us, event | category | flops | bytes accessed | tf_op | source)
XLA Modules:
  0.0 354.5 jit_solution(2730051306671288347)
XLA Ops:
  7.2 0.0 all-gather.7.cloned.1.call-start
  7.2 0.7 all-gather.7.cloned.1.call-update
  7.9 0.0 all-gather.5.cloned.1.call-start
  7.9 0.7 all-gather.5.cloned.1.call-update
  8.6 0.0 reduce-scatter.5.cloned.1.call-start
  8.7 0.1 iota_add_fusion
  8.8 0.1 add.96
  8.9 0.7 broadcast_multiply_fusion.2
  9.5 0.7 broadcast_compare_fusion.1
  10.3 0.7 broadcast_compare_fusion
  11.0 28.5 %all-gather.7.cloned.1.call-done = bf16[5,256,1024]{2,1,0:T(8,128)(2,1)} async-done(((bf16[5,32,1024]{2,1,0:T(8,128)(2,1)}), bf16[5,256,1024]{2,1,0:T(8,128)(2,1)}) %all-gather.7.cloned.1.call-update) | async-done | bytes 2621456 | tf_op jit(solution)/shard_map/all_gather | solution.py:27
  39.4 58.8 %all-gather.5.cloned.1.call-done = bf16[5,512,1024]{2,1,0:T(8,128)(2,1)} async-done(((bf16[5,32,1024]{2,1,0:T(8,128)(2,1)}), bf16[5,512,1024]{2,1,0:T(8,128)(2,1)}) %all-gather.5.cloned.1.call-update) | async-done | bytes 5242896 | tf_op jit(solution)/shard_map/all_gather | solution.py:26
  98.2 0.0 copy-start.3
  98.2 4.9 %fusion.6 = (f32[5,512]{1,0:T(8,128)S(1)}, f32[5,256]{1,0:T(8,128)S(1)}, f32[5,512,256]{2,1,0:T(8,128)S(1)}) fusion(pred[5,256]{1,0:T(8,128)(4,1)S(1)} %broadcast_compare_fusion.1, pred[5,512]{1,0:T(8,128)(4,1)S(1)} %broadcast_compare_fusion, bf16[5,512,1024]{2,1,0:T(8,128)(2,1)} %all-gather.5.cloned.1.call-done, ...), kind=kOutput, calls=%fused_computation.13 | convolution fusion | flops 1345450240 | bytes 10504960 | tf_op jit(solution)/shard_map/prd,pcd->prc/dot_general | solution.py:37
  103.2 0.0 copy-start.2
  103.2 2.0 fusion
  105.2 13.6 %all-gather.1 = f32[16,5,256]{2,1,0:T(8,128)S(1)} all-gather(f32[2,5,256]{2,1,0:T(8,128)S(1)} %pad_maximum_fusion.1), channel_id=3, replica_groups=mesh['dp'=8,'pair'=16] {'dp'}, dimensions={0}, use_global_device_ids=true | all-gather | bytes 92160 | tf_op jit(solution)/shard_map/all_gather | solution.py:46
  118.9 0.0 copy-done.2
  118.9 0.1 add_select_fusion.1
  119.0 18.7 %all-gather = f32[32,5,512]{2,1,0:T(8,128)S(1)} all-gather(f32[2,5,512]{2,1,0:T(8,128)S(1)} %pad_maximum_fusion), channel_id=2, replica_groups=mesh['dp'=8,'pair'=16] {'pair'}, dimensions={0}, use_global_device_ids=true | all-gather | bytes 348160 | tf_op jit(solution)/shard_map/all_gather | solution.py:45
  137.7 0.1 fusion.13
  137.8 0.1 add_select_fusion
  137.8 0.0 copy-done.3
  137.8 5.1 %broadcast_multiply_fusion.1 = f32[5,256,1024]{2,1,0:T(8,128)} fusion(bf16[5,512,1024]{2,1,0:T(8,128)(2,1)S(1)} %copy-done.3, f32[5,512,256]{2,1,0:T(8,128)S(1)} %get-tuple-element.12, f32[5,256]{1,0:T(8,128)S(1)} %add_select_fusion.1, f32[5,512]{1,0:T(8,128)S(1)} %add_select_fusion, f32[5]{0:T(128)S(1)} %get-tuple-element.11, ...), kind=kOutput, calls=%fused_computation.11 | convolution fusion | flops 1349386240 | bytes 13126420 | tf_op jit(solution)/shard_map/prc,prd->pcd/dot_general | solution.py:68
  142.9 0.0 reduce-scatter.5.cloned.1.call-update
  142.9 0.0 reduce-scatter.3.cloned.1.call-start
  143.0 7.6 %broadcast_multiply_fusion = f32[5,512,1024]{2,1,0:T(8,128)} fusion(bf16[5,256,1024]{2,1,0:T(8,128)(2,1)} %all-gather.7.cloned.1.call-done, f32[5,512,256]{2,1,0:T(8,128)S(1)} %get-tuple-element.12, f32[5,256]{1,0:T(8,128)S(1)} %add_select_fusion.1, f32[5,512]{1,0:T(8,128)S(1)} %add_select_fusion, f32[5]{0:T(128)S(1)} %get-tuple-element.11, ...), kind=kOutput, calls=%fused_computation.5 | convolution fusion | flops 1350696960 | bytes 15747860 | tf_op jit(solution)/shard_map/prc,pcd->prd/dot_general | solution.py:64
  150.5 0.0 copy-start
  150.5 0.0 copy-start.1
  150.6 0.0 reduce-scatter.3.cloned.1.call-update
  150.6 0.1 broadcast_compare_fusion.2
  150.7 32.2 %reduce-scatter.5.cloned.1.call-done = f32[5,32,1024]{2,1,0:T(8,128)} async-done(((f32[5,256,1024]{2,1,0:T(8,128)}), f32[5,32,1024]{2,1,0:T(8,128)}) %reduce-scatter.5.cloned.1.call-update) | async-done | bytes 655376 | tf_op jit(solution)/shard_map/reduce_scatter | solution.py:72
  182.9 94.8 %reduce-scatter.3.cloned.1.call-done = f32[5,32,1024]{2,1,0:T(8,128)} async-done(((f32[5,512,1024]{2,1,0:T(8,128)}), f32[5,32,1024]{2,1,0:T(8,128)}) %reduce-scatter.3.cloned.1.call-update) | async-done | bytes 655376 | tf_op jit(solution)/shard_map/reduce_scatter | solution.py:71
  277.7 0.0 copy-done
  277.7 0.0 copy-done.1
  277.7 2.7 fusion.8
  280.4 0.2 select_reduce_fusion
  280.6 65.0 %psum.7 = f32[5]{0:T(128)S(1)} all-reduce(f32[5]{0:T(128)S(1)} %select_reduce_fusion), channel_id=1, replica_groups=mesh['dp'=8,'pair'=16] {'dp','pair'}, use_global_device_ids=true, to_apply=%region_10.11 | all-reduce | flops 5 | bytes 40 | tf_op jit(solution)/shard_map/psum | solution.py:58
  345.6 0.6 fusion.18
  (8 shorter events, 0.1 us)
Async XLA Ops:
  7.2 32.3 %all-gather.7.cloned.1.call-start = ((), (), s32[]{:S(2)}) async-start(), calls=%async_computation.3 | async-start | bytes 2949120 | tf_op jit(solution)/shard_map/all_gather | solution.py:27
  7.9 90.3 %all-gather.5.cloned.1.call-start = ((), (), s32[]{:S(2)}) async-start(), calls=%async_computation.2 | async-start | bytes 5570560 | tf_op jit(solution)/shard_map/all_gather | solution.py:26
  8.6 174.2 %reduce-scatter.5.cloned.1.call-start = ((), (), s32[]{:S(2)}) async-start(), calls=%async_computation.5 | async-start | bytes 5898240 | tf_op jit(solution)/shard_map/reduce_scatter | solution.py:72
  98.2 39.6 %copy-start.3 = (bf16[5,512,1024]{2,1,0:T(8,128)(2,1)S(1)}, bf16[5,512,1024]{2,1,0:T(8,128)(2,1)}, u32[]{:S(2)}) copy-start(bf16[5,512,1024]{2,1,0:T(8,128)(2,1)} %all-gather.5.cloned.1.call-done) | copy-start | bytes 15728644
  103.2 15.7 %copy-start.2 = (s32[5]{0:T(128)S(1)}, s32[5]{0:T(128)}, u32[]{:S(2)}) copy-start(s32[5]{0:T(128)} %param.6) | copy-start | bytes 64
  142.9 134.8 %reduce-scatter.3.cloned.1.call-start = ((), (), s32[]{:S(2)}) async-start(), calls=%async_computation.4 | async-start | bytes 11141120 | tf_op jit(solution)/shard_map/reduce_scatter | solution.py:71
  150.5 127.1 %copy-start = (bf16[5,32,1024]{2,1,0:T(8,128)(2,1)S(1)}, bf16[5,32,1024]{2,1,0:T(8,128)(2,1)}, u32[]{:S(2)}) copy-start(bf16[5,32,1024]{2,1,0:T(8,128)(2,1)} %param.5) | copy-start | bytes 983044
  150.5 127.1 %copy-start.1 = (bf16[5,32,1024]{2,1,0:T(8,128)(2,1)S(1)}, bf16[5,32,1024]{2,1,0:T(8,128)(2,1)}, u32[]{:S(2)}) copy-start(bf16[5,32,1024]{2,1,0:T(8,128)(2,1)} %param.4) | copy-start | bytes 983044
Sparse Core Ops, SparseCore 0:
  9.7 29.7 all-gather.6
  41.6 56.6 all-gather.4
  143.0 39.7 reduce-scatter.4
  186.2 91.4 reduce-scatter.2
where the time goes:
time: 355 us
  waiting for transfers between devices  216 us (61%)
  blocking collectives  97.3 us (27%)
  matrix products  17.6 us (5%)
  between operations  15.6 us (4%)
  other arithmetic  8.11 us (2%)
    reduce_scatter x1, waiting for transfers between devices, per_device(): lax.psum_scatter(grad_rows, 'pair', scatter_dimension=1, tiled=True)  94.8 us
    psum x1, blocking collectives, per_device(): totals = lax.psum(jnp.sum(loss_terms, axis=1), ('dp', 'pair'))  65 us
    all_gather x1, waiting for transfers between devices, per_device(): row_set = lax.all_gather(anchor, 'pair', axis=1, tiled=True)  58.8 us
    reduce_scatter x1, waiting for transfers between devices, per_device(): lax.psum_scatter(grad_cols, 'dp', scatter_dimension=1, tiled=True)  32.2 us
    all_gather x1, waiting for transfers between devices, per_device(): col_set = lax.all_gather(partner, 'dp', axis=1, tiled=True)  28.5 us
    all_gather x1, blocking collectives, per_device(): row_stats = lax.all_gather(jnp.stack([row_high, row_sum]), 'pair')  18.7 us
    all_gather x1, blocking collectives, per_device(): col_stats = lax.all_gather(jnp.stack([col_high, col_sum]), 'dp')  13.6 us
    dot_general x1, matrix products, per_device(): jnp.einsum('prc,pcd->prd', weights, col_set, preferred_element_type=jnp.f...  7.57 us
  transfers between devices with their start and end apart: 4, of which 4 were waited for; matrix products, arithmetic and copies ran while one was open for 3% of the time, Pallas kernels for 0%

commit v1 on v0

--- a/solution.py
+++ b/solution.py
@@ -24,7 +24,12 @@
     pair_place = lax.axis_index("pair")
     own_first = (dp_index * pair_size + pair_place) * shard_rows
     row_set = lax.all_gather(anchor, "pair", axis=1, tiled=True)
-    col_set = lax.all_gather(partner, "dp", axis=1, tiled=True)
+    ring = [partner]
+    for hop in range(7):
+        ring.append(lax.ppermute(ring[-1], "dp", [(dev, (dev + 1) % 8) for dev in range(8)]))
+    col_set = jnp.roll(
+        jnp.concatenate(ring[::-1], axis=1), (lax.axis_index("dp") + 1) * ring[0].shape[1], axis=1
+    )
     row_count = row_set.shape[1]
     offsets = jnp.arange(shard_rows, dtype=jnp.int32)
     row_global = dp_index * row_count + jnp.arange(row_count, dtype=jnp.int32)

time: 355 us -> 334 us (0.941)
  waiting for transfers between devices: 216 us -> 159 us
  starting transfers between devices: 0.16 us -> 14.8 us
  local copies, waits for them, and re-layouts: 0.1 us -> 13.1 us
  blocking collectives: 97.3 us -> 105 us
    all_gather x1, waiting for transfers between devices: 58.8 us -> 0.01 us  [per_device(): row_set = lax.all_gather(anchor, 'pair', axis=1, tiled=True)]
    ppermute x0 -> x7, waiting for transfers between devices: none -> 32.1 us  [per_device(): lax.ppermute(ring[-1], 'dp', [(dev, (dev + 1) % 8) for dev in range(8)])]
    all_gather x1 -> x0, waiting for transfers between devices: 28.5 us -> none  [per_device(): col_set = lax.all_gather(partner, 'dp', axis=1, tiled=True)]
    ppermute x0 -> x7, starting transfers between devices: none -> 14.6 us  [per_device(): lax.ppermute(ring[-1], 'dp', [(dev, (dev + 1) % 8) for dev in range(8)])]
    unnamed x8 -> x23, local copies, waits for them, and re-layouts: 0.02 us -> 12.3 us
    all_gather x1, blocking collectives: 13.6 us -> 19.2 us  [per_device(): col_stats = lax.all_gather(jnp.stack([col_high, col_sum]), 'dp')]
  transfers between devices with their start and end apart: 4 -> 10, of which waited for: 4 -> 9; matrix products, arithmetic and copies ran while one was open for 3% -> 7% of each run, Pallas kernels for 0% -> 0%
where the time goes in v1:
time: 334 us
  waiting for transfers between devices  159 us (48%)
  blocking collectives  105 us (31%)
  matrix products  18.7 us (6%)
  between operations  15.6 us (5%)
  starting transfers between devices  14.8 us (4%)
  local copies, waits for them, and re-layouts  13.1 us (4%)
  other arithmetic  8 us (2%)
    reduce_scatter x1, waiting for transfers between devices, per_device(): lax.psum_scatter(grad_rows, 'pair', scatter_dimension=1, tiled=True)  94.8 us
    psum x1, blocking collectives, per_device(): totals = lax.psum(jnp.sum(loss_terms, axis=1), ('dp', 'pair'))  65.1 us
    ppermute x7, waiting for transfers between devices, per_device(): lax.ppermute(ring[-1], 'dp', [(dev, (dev + 1) % 8) for dev in range(8)])  32.1 us
    reduce_scatter x1, waiting for transfers between devices, per_device(): lax.psum_scatter(grad_cols, 'dp', scatter_dimension=1, tiled=True)  31.4 us
    all_gather x1, blocking collectives, per_device(): row_stats = lax.all_gather(jnp.stack([row_high, row_sum]), 'pair')  20.4 us
    all_gather x1, blocking collectives, per_device(): col_stats = lax.all_gather(jnp.stack([col_high, col_sum]), 'dp')  19.2 us
    ppermute x7, starting transfers between devices, per_device(): lax.ppermute(ring[-1], 'dp', [(dev, (dev + 1) % 8) for dev in range(8)])  14.6 us
    unnamed x23, local copies, waits for them, and re-layouts  12.3 us
  transfers between devices with their start and end apart: 10, of which 9 were waited for; matrix products, arithmetic and copies ran while one was open for 7% of the time, Pallas kernels for 0%

profile of v1, /device:TPU:1, one launch (start us, length us, event | category | flops | bytes accessed | tf_op | source)
XLA Modules:
  0.0 333.8 jit_solution(8632040423517312908)
XLA Ops:
  7.2 0.0 copy-start
  7.2 0.0 all-gather.4.cloned.1.call-start
  7.2 0.7 all-gather.4.cloned.1.call-update
  7.9 0.0 reduce-scatter.5.cloned.1.call-start
  8.0 2.6 collective-permute-start
  10.6 4.3 %collective-permute-done = bf16[5,32,1024]{2,1,0:T(8,128)(2,1)S(1)} collective-permute-done((bf16[5,32,1024]{2,1,0:T(8,128)(2,1)}, bf16[5,32,1024]{2,1,0:T(8,128)(2,1)S(1)}, u32[]{:S(2)}, u32[]{:S(2)}) %collective-permute-start) | collective-permute-done | bytes 327712 | tf_op jit(solution)/shard_map/ppermute | solution.py:29
  14.9 2.4 collective-permute-start.1
  17.3 4.0 %collective-permute-done.1 = bf16[5,32,1024]{2,1,0:T(8,128)(2,1)S(1)} collective-permute-done((bf16[5,32,1024]{2,1,0:T(8,128)(2,1)S(1)}, bf16[5,32,1024]{2,1,0:T(8,128)(2,1)S(1)}, u32[]{:S(2)}, u32[]{:S(2)}) %collective-permute-start.1) | collective-permute-done | bytes 327712 | tf_op jit(solution)/shard_map/ppermute | solution.py:29
  21.3 2.5 collective-permute-start.2
  23.8 4.0 %collective-permute-done.2 = bf16[5,32,1024]{2,1,0:T(8,128)(2,1)S(1)} collective-permute-done((bf16[5,32,1024]{2,1,0:T(8,128)(2,1)S(1)}, bf16[5,32,1024]{2,1,0:T(8,128)(2,1)S(1)}, u32[]{:S(2)}, u32[]{:S(2)}) %collective-permute-start.2) | collective-permute-done | bytes 327712 | tf_op jit(solution)/shard_map/ppermute | solution.py:29
  27.8 2.5 collective-permute-start.3
  30.3 4.0 %collective-permute-done.3 = bf16[5,32,1024]{2,1,0:T(8,128)(2,1)S(1)} collective-permute-done((bf16[5,32,1024]{2,1,0:T(8,128)(2,1)S(1)}, bf16[5,32,1024]{2,1,0:T(8,128)(2,1)S(1)}, u32[]{:S(2)}, u32[]{:S(2)}) %collective-permute-start.3) | collective-permute-done | bytes 327712 | tf_op jit(solution)/shard_map/ppermute | solution.py:29
  34.3 2.5 collective-permute-start.4
  36.8 0.1 iota_add_fusion
  36.9 4.7 %collective-permute-done.4 = bf16[5,32,1024]{2,1,0:T(8,128)(2,1)S(1)} collective-permute-done((bf16[5,32,1024]{2,1,0:T(8,128)(2,1)S(1)}, bf16[5,32,1024]{2,1,0:T(8,128)(2,1)S(1)}, u32[]{:S(2)}, u32[]{:S(2)}) %collective-permute-start.4) | collective-permute-done | bytes 327712 | tf_op jit(solution)/shard_map/ppermute | solution.py:29
  41.6 1.7 collective-permute-start.5
  43.3 0.7 broadcast_multiply_fusion.2
  43.9 0.1 add.109
  44.0 0.7 broadcast_compare_fusion.1
  44.7 4.5 %collective-permute-done.5 = bf16[5,32,1024]{2,1,0:T(8,128)(2,1)S(1)} collective-permute-done((bf16[5,32,1024]{2,1,0:T(8,128)(2,1)S(1)}, bf16[5,32,1024]{2,1,0:T(8,128)(2,1)S(1)}, u32[]{:S(2)}, u32[]{:S(2)}) %collective-permute-start.5) | collective-permute-done | bytes 327712 | tf_op jit(solution)/shard_map/ppermute | solution.py:29
  49.3 0.5 collective-permute-start.6
  49.8 0.7 broadcast_compare_fusion
  50.5 6.5 %collective-permute-done.6 = bf16[5,32,1024]{2,1,0:T(8,128)(2,1)S(1)} collective-permute-done((bf16[5,32,1024]{2,1,0:T(8,128)(2,1)S(1)}, bf16[5,32,1024]{2,1,0:T(8,128)(2,1)S(1)}, u32[]{:S(2)}, u32[]{:S(2)}) %collective-permute-start.6) | collective-permute-done | bytes 327712 | tf_op jit(solution)/shard_map/ppermute | solution.py:29
  57.0 0.8 constant_dynamic-update-slice_fusion.15
  57.7 0.7 constant_dynamic-update-slice_fusion.14
  58.5 0.7 constant_dynamic-update-slice_fusion.13
  59.2 0.8 constant_dynamic-update-slice_fusion.12
  60.0 0.7 constant_dynamic-update-slice_fusion.11
  60.7 0.8 constant_dynamic-update-slice_fusion.10
  61.5 0.7 constant_dynamic-update-slice_fusion.9
  62.2 1.7 constant_dynamic-update-slice_fusion.8
  64.0 0.7 constant_dynamic-update-slice_fusion.7
  64.7 0.7 constant_dynamic-update-slice_fusion.6
  65.4 0.8 constant_dynamic-update-slice_fusion.5
  66.2 0.8 constant_dynamic-update-slice_fusion.4
  67.0 0.8 constant_dynamic-update-slice_fusion.3
  67.7 0.8 constant_dynamic-update-slice_fusion.2
  68.5 0.8 constant_dynamic-update-slice_fusion.1
  69.2 0.0 copy-done
  69.2 0.8 constant_dynamic-update-slice_fusion
  70.0 0.0 all-gather.4.cloned.1.call-done
  70.0 0.0 copy-start.3
  70.0 5.3 %fusion.11 = (f32[5,512]{1,0:T(8,128)S(1)}, f32[5,256]{1,0:T(8,128)S(1)}, f32[5,256,512]{2,1,0:T(8,128)S(1)}) fusion(pred[5,256]{1,0:T(8,128)(4,1)S(1)} %broadcast_compare_fusion.1, pred[5,512]{1,0:T(8,128)(4,1)S(1)} %broadcast_compare_fusion, bf16[5,512,1024]{2,1,0:T(8,128)(2,1)} %all-gather.4.cloned.1.call-done, ...), kind=kOutput, calls=%fused_computation.20 | convolution fusion | flops 1345450240 | bytes 10504964 | tf_op jit(solution)/shard_map/prd,pcd->prc/dot_general | solution.py:42
  75.4 1.9 fusion
  77.3 19.2 %all-gather.1 = f32[16,5,256]{2,1,0:T(8,128)S(1)} all-gather(f32[2,5,256]{2,1,0:T(8,128)S(1)} %pad_maximum_fusion.1), channel_id=3, replica_groups=mesh['dp'=8,'pair'=16] {'dp'}, dimensions={0}, use_global_device_ids=true | all-gather | bytes 92160 | tf_op jit(solution)/shard_map/all_gather | solution.py:51
  96.5 0.0 copy-done.2
  96.5 0.1 add_select_fusion.1
  96.6 20.4 %all-gather = f32[32,5,512]{2,1,0:T(8,128)S(1)} all-gather(f32[2,5,512]{2,1,0:T(8,128)S(1)} %pad_maximum_fusion), channel_id=2, replica_groups=mesh['dp'=8,'pair'=16] {'pair'}, dimensions={0}, use_global_device_ids=true | all-gather | bytes 348160 | tf_op jit(solution)/shard_map/all_gather | solution.py:50
  117.1 0.1 fusion.18
  117.1 0.1 add_select_fusion
  117.2 0.0 copy-done.3
  117.2 5.1 %broadcast_multiply_fusion.1 = f32[5,256,1024]{2,1,0:T(8,128)} fusion(bf16[5,512,1024]{2,1,0:T(8,128)(2,1)S(1)} %copy-done.3, f32[5,256,512]{2,1,0:T(8,128)S(1)} %get-tuple-element.12, f32[5,256]{1,0:T(8,128)S(1)} %add_select_fusion.1, f32[5,512]{1,0:T(8,128)S(1)} %add_select_fusion, f32[5]{0:T(128)S(1)} %get-tuple-element.11, ...), kind=kOutput, calls=%fused_computation.15 | convolution fusion | flops 1349386240 | bytes 13126420 | tf_op jit(solution)/shard_map/prc,prd->pcd/dot_general | solution.py:73
  122.3 0.0 reduce-scatter.5.cloned.1.call-update
  122.3 0.0 reduce-scatter.3.cloned.1.call-start
  122.4 8.3 %broadcast_multiply_fusion = f32[5,512,1024]{2,1,0:T(8,128)} fusion(bf16[5,512,1024]{2,1,0:T(8,128)(2,1)} %constant_dynamic-update-slice_fusion, s32[]{:T(128)S(6)} %select_n.77, f32[5,256,512]{2,1,0:T(8,128)S(1)} %get-tuple-element.12, f32[5,256]{1,0:T(8,128)S(1)} %add_select_fusion.1, f32[5,512]{1,0:T(8,128)S(1)} %add_select_fusion, ...), kind=kOutput, calls=%fused_computation.5 | convolution fusion | flops 1350696960 | bytes 15747864 | tf_op jit(solution)/shard_map/prc,pcd->prd/dot_general | solution.py:69
  130.6 0.0 reduce-scatter.3.cloned.1.call-update
  130.7 0.1 broadcast_compare_fusion.2
  130.7 31.4 %reduce-scatter.5.cloned.1.call-done = f32[5,32,1024]{2,1,0:T(8,128)} async-done(((f32[5,256,1024]{2,1,0:T(8,128)}), f32[5,32,1024]{2,1,0:T(8,128)}) %reduce-scatter.5.cloned.1.call-update) | async-done | bytes 655376 | tf_op jit(solution)/shard_map/reduce_scatter | solution.py:77
  162.1 94.8 %reduce-scatter.3.cloned.1.call-done = f32[5,32,1024]{2,1,0:T(8,128)} async-done(((f32[5,512,1024]{2,1,0:T(8,128)}), f32[5,32,1024]{2,1,0:T(8,128)}) %reduce-scatter.3.cloned.1.call-update) | async-done | bytes 655376 | tf_op jit(solution)/shard_map/reduce_scatter | solution.py:76
  256.9 0.0 copy-done.1
  256.9 2.7 fusion.13
  259.7 0.2 select_reduce_fusion
  259.8 65.1 %psum.7 = f32[5]{0:T(128)S(1)} all-reduce(f32[5]{0:T(128)S(1)} %select_reduce_fusion), channel_id=1, replica_groups=mesh['dp'=8,'pair'=16] {'dp','pair'}, use_global_device_ids=true, to_apply=%region_10.11 | all-reduce | flops 5 | bytes 40 | tf_op jit(solution)/shard_map/psum | solution.py:63
  324.9 0.6 fusion.25
  (10 shorter events, 0.1 us)
Async XLA Ops:
  7.2 62.1 %copy-start = (bf16[5,32,1024]{2,1,0:T(8,128)(2,1)S(1)}, bf16[5,32,1024]{2,1,0:T(8,128)(2,1)}, u32[]{:S(2)}) copy-start(bf16[5,32,1024]{2,1,0:T(8,128)(2,1)} %param.5) | copy-start | bytes 983044
  7.2 62.8 %all-gather.4.cloned.1.call-start = ((), (), s32[]{:S(2)}) async-start(), calls=%async_computation.2 | async-start | bytes 5570560 | tf_op jit(solution)/shard_map/all_gather | solution.py:26
  7.9 154.2 %reduce-scatter.5.cloned.1.call-start = ((), (), s32[]{:S(2)}) async-start(), calls=%async_computation.4 | async-start | bytes 5898240 | tf_op jit(solution)/shard_map/reduce_scatter | solution.py:77
  8.0 6.9 %collective-permute-start = (bf16[5,32,1024]{2,1,0:T(8,128)(2,1)}, bf16[5,32,1024]{2,1,0:T(8,128)(2,1)S(1)}, u32[]{:S(2)}, u32[]{:S(2)}) collective-permute-start(bf16[5,32,1024]{2,1,0:T(8,128)(2,1)} %param.5), channel_id=1, source_target_pairs={{0,16},{16,32},{32,48},{48,64},{64,80},{80,96},{96,112},{112,0},{1... | collective-permute-start | bytes 983048 | tf_op jit(solution)/shard_map/ppermute | solution.py:29
  14.9 6.4 %collective-permute-start.1 = (bf16[5,32,1024]{2,1,0:T(8,128)(2,1)S(1)}, bf16[5,32,1024]{2,1,0:T(8,128)(2,1)S(1)}, u32[]{:S(2)}, u32[]{:S(2)}) collective-permute-start(bf16[5,32,1024]{2,1,0:T(8,128)(2,1)S(1)} %collective-permute-done), channel_id=1, source_target_pairs={{0,16},{16,32},{32,48},{48,64},{64,80},{80,96},{96,112},{112,0},{1... | collective-permute-start | bytes 983048 | tf_op jit(solution)/shard_map/ppermute | solution.py:29
  21.3 6.5 %collective-permute-start.2 = (bf16[5,32,1024]{2,1,0:T(8,128)(2,1)S(1)}, bf16[5,32,1024]{2,1,0:T(8,128)(2,1)S(1)}, u32[]{:S(2)}, u32[]{:S(2)}) collective-permute-start(bf16[5,32,1024]{2,1,0:T(8,128)(2,1)S(1)} %collective-permute-done.1), channel_id=1, source_target_pairs={{0,16},{16,32},{32,48},{48,64},{64,80},{80,96},{96,112},{112,0},{1... | collective-permute-start | bytes 983048 | tf_op jit(solution)/shard_map/ppermute | solution.py:29
  27.8 6.5 %collective-permute-start.3 = (bf16[5,32,1024]{2,1,0:T(8,128)(2,1)S(1)}, bf16[5,32,1024]{2,1,0:T(8,128)(2,1)S(1)}, u32[]{:S(2)}, u32[]{:S(2)}) collective-permute-start(bf16[5,32,1024]{2,1,0:T(8,128)(2,1)S(1)} %collective-permute-done.2), channel_id=1, source_target_pairs={{0,16},{16,32},{32,48},{48,64},{64,80},{80,96},{96,112},{112,0},{1... | collective-permute-start | bytes 983048 | tf_op jit(solution)/shard_map/ppermute | solution.py:29
  34.3 7.3 %collective-permute-start.4 = (bf16[5,32,1024]{2,1,0:T(8,128)(2,1)S(1)}, bf16[5,32,1024]{2,1,0:T(8,128)(2,1)S(1)}, u32[]{:S(2)}, u32[]{:S(2)}) collective-permute-start(bf16[5,32,1024]{2,1,0:T(8,128)(2,1)S(1)} %collective-permute-done.3), channel_id=1, source_target_pairs={{0,16},{16,32},{32,48},{48,64},{64,80},{80,96},{96,112},{112,0},{1... | collective-permute-start | bytes 983048 | tf_op jit(solution)/shard_map/ppermute | solution.py:29
  41.6 7.7 %collective-permute-start.5 = (bf16[5,32,1024]{2,1,0:T(8,128)(2,1)S(1)}, bf16[5,32,1024]{2,1,0:T(8,128)(2,1)S(1)}, u32[]{:S(2)}, u32[]{:S(2)}) collective-permute-start(bf16[5,32,1024]{2,1,0:T(8,128)(2,1)S(1)} %collective-permute-done.4), channel_id=1, source_target_pairs={{0,16},{16,32},{32,48},{48,64},{64,80},{80,96},{96,112},{112,0},{1... | collective-permute-start | bytes 983048 | tf_op jit(solution)/shard_map/ppermute | solution.py:29
  49.3 7.7 %collective-permute-start.6 = (bf16[5,32,1024]{2,1,0:T(8,128)(2,1)S(1)}, bf16[5,32,1024]{2,1,0:T(8,128)(2,1)S(1)}, u32[]{:S(2)}, u32[]{:S(2)}) collective-permute-start(bf16[5,32,1024]{2,1,0:T(8,128)(2,1)S(1)} %collective-permute-done.5), channel_id=1, source_target_pairs={{0,16},{16,32},{32,48},{48,64},{64,80},{80,96},{96,112},{112,0},{1... | collective-permute-start | bytes 983048 | tf_op jit(solution)/shard_map/ppermute | solution.py:29
  70.0 26.5 %copy-start.2 = (s32[5]{0:T(128)S(1)}, s32[5]{0:T(128)}, u32[]{:S(2)}) copy-start(s32[5]{0:T(128)} %param.6) | copy-start | bytes 64
  70.0 47.2 %copy-start.3 = (bf16[5,512,1024]{2,1,0:T(8,128)(2,1)S(1)}, bf16[5,512,1024]{2,1,0:T(8,128)(2,1)}, u32[]{:S(2)}) copy-start(bf16[5,512,1024]{2,1,0:T(8,128)(2,1)} %all-gather.4.cloned.1.call-done) | copy-start | bytes 15728644
  122.3 134.6 %reduce-scatter.3.cloned.1.call-start = ((), (), s32[]{:S(2)}) async-start(), calls=%async_computation.3 | async-start | bytes 11141120 | tf_op jit(solution)/shard_map/reduce_scatter | solution.py:76
  130.6 126.3 %copy-start.1 = (bf16[5,32,1024]{2,1,0:T(8,128)(2,1)S(1)}, bf16[5,32,1024]{2,1,0:T(8,128)(2,1)}, u32[]{:S(2)}) copy-start(bf16[5,32,1024]{2,1,0:T(8,128)(2,1)} %param.4) | copy-start | bytes 983044
Sparse Core Ops, SparseCore 0:
  10.2 59.6 all-gather.3
  122.4 39.6 reduce-scatter.4
  165.6 91.3 reduce-scatter.2
